TPU v7x, 512 devices: a whole 4x8x8 slice. The times are simulated.
512 devices in a mesh: section: 64 (over y_hi, z, x), rep: 8 (over y_lo, core).
Axes of the slice: x: 4, y: 8 (y_hi: 2, y_lo: 4; y = y_hi * 4 + y_lo), z: 8, core: 2. Of those that a mesh axis runs over, the one named last changes fastest.
Arguments:
- features: bfloat16 [65536, 512], P(('section', 'rep')), may hold values from -6 to 6
- col_panels: int32 [512, 8, 12], P('section', 'rep'), may hold values from 0 to 511, as said below
- block_counts: int32 [512, 8], P('section', 'rep'), may hold values from 1 to 12, as said below
- block_values: bfloat16 [512, 8, 12, 128, 128], P('section', 'rep'), may hold values from 0.0019989014 to 0.019897461
- weight: bfloat16 [512, 512], replicated, may hold values from -0.25 to 0.25
- bias: float32 [512], replicated, may hold values from -3 to 3
- cotangent: bfloat16 [65536, 512], P(('section', 'rep')), may hold values from -6 to 6
Outputs:
- hidden: bfloat16 [65536, 512], P(('section', 'rep'))
- weight_grad: float32 [512, 512], replicated
- bias_grad: float32 [512], replicated
Inputs may be any that keep to these rules, and one draw needn't show every extreme that they name: Column group r holds the column panels c with (c) % 8 == r; col_panels[p, r, k] lies in column group r, and the 12 entries of one list are distinct. Only the first block_counts[p, r] slots of a list are nonzero blocks; later slots are ignored. The count 12 occurs in every draw.
All inputs are finite; a program needn't handle non-finite values.
Results may differ from a plain program's by a relative error of at most 0.0055.
Values may be sent and summed in bfloat16 or wider, within the bound.
No kernel may reach another device: no remote copies, remote signals or barrier semaphores. Data moves between devices by JAX's collectives and lax.ppermute only.
A program may use at most 64 MiB of HBM per device.

v0:
```python
import math
import jax
import jax.numpy as jnp
from jax import lax
from jax.sharding import PartitionSpec as P


def shards(features, col_panels, block_counts, block_values, weight, bias, cotangent):
    rep_count = lax.axis_size("rep")
    rep_index = lax.axis_index("rep")
    tile_size = block_values.shape[-1]
    feat_width = features.shape[1]
    own_panels = features.shape[0] // tile_size
    row_panels = col_panels.shape[0]
    slot_count = col_panels.shape[2]
    global_cols = col_panels[:, 0, :]
    local_cols = global_cols // (own_panels * rep_count) * own_panels + global_cols % own_panels
    live_counts = block_counts[:, 0]
    slot_mask = jnp.arange(slot_count, dtype=jnp.int32)[None, :] < live_counts[:, None]
    tiles = block_values[:, 0]
    empty = jnp.zeros((row_panels, tile_size, feat_width), jnp.float32)
    gathered = lax.all_gather(features, "section", axis=0, tiled=True)
    all_panels = gathered.reshape(-1, tile_size, feat_width)
    slot_step = 4
    turn_count = (jnp.max(live_counts) + slot_step - 1) // slot_step

    def one_turn(turn, running):
        begin_slot = turn * slot_step
        step_cols = lax.dynamic_slice_in_dim(local_cols, begin_slot, slot_step, 1)
        step_mask = lax.dynamic_slice_in_dim(slot_mask, begin_slot, slot_step, 1)
        step_tiles = lax.dynamic_slice_in_dim(tiles, begin_slot, slot_step, 1)
        step_tiles = jnp.where(step_mask[:, :, None, None], step_tiles, jnp.zeros((), jnp.bfloat16))
        picked = all_panels[step_cols]
        return running + jnp.einsum(
            "gkab,gkbf->gaf", step_tiles, picked, preferred_element_type=jnp.float32
        )

    gathered_sum = lax.fori_loop(0, turn_count, one_turn, empty)
    partial_value = gathered_sum.reshape(row_panels * tile_size, feat_width)
    own_rows = own_panels * tile_size
    summed_all = lax.psum(partial_value, "rep")
    summed_own = lax.dynamic_slice_in_dim(summed_all, rep_index * own_rows, own_rows, 0)
    aggregated = summed_own.astype(jnp.bfloat16)
    pre = jnp.dot(aggregated, weight, preferred_element_type=jnp.float32) + bias
    hidden = jax.nn.silu(pre).astype(jnp.bfloat16)
    sigmoid_pre = jax.nn.sigmoid(pre)
    slope = (
        cotangent.astype(jnp.float32) * (sigmoid_pre * (1.0 + pre * (1.0 - sigmoid_pre)))
    ).astype(jnp.bfloat16)
    local_weight = jnp.einsum("nd,nf->df", aggregated, slope, preferred_element_type=jnp.float32)
    local_bias = jnp.sum(slope.astype(jnp.float32), axis=0)
    weight_sum, bias_sum = lax.psum((local_weight, local_bias), ("section", "rep"))
    node_total = lax.axis_size("section") * rep_count * own_rows
    factor = 1.0 / math.sqrt(node_total)
    return (hidden, weight_sum * factor, bias_sum * factor)


def solution(mesh):
    in_specs = (
        P(("section", "rep"), None),
        P("section", "rep", None),
        P("section", "rep"),
        P("section", "rep", None, None, None),
        P(),
        P(),
        P(("section", "rep"), None),
    )
    out_specs = (P(("section", "rep"), None), P(), P())
    return jax.shard_map(shards, mesh=mesh, in_specs=in_specs, out_specs=out_specs, check_vma=False)
```

profile of v0, /device:TPU:24, one launch (start us, length us, event | category | flops | bytes accessed | tf_op | source)
XLA Modules:
  0.0 583.3 jit_solution(16949796323749232449)
XLA Ops:
  7.2 0.0 all-gather.2.cloned.1.call-start
  7.2 0.7 all-gather.2.cloned.1.call-update
  7.9 0.0 all-reduce.3.cloned.1.call-start
  8.0 1.3 reduce_max.9
  9.9 0.7 iota_compare_fusion
  10.7 0.7 add_select_fusion
  11.4 185.0 %all-gather.2.cloned.1.call-done = bf16[8192,512]{1,0:T(8,128)(2,1)} async-done(((bf16[128,512]{1,0:T(8,128)(2,1)}), bf16[8192,512]{1,0:T(8,128)(2,1)}) %all-gather.2.cloned.1.call-update) | async-done | bytes 8388624 | tf_op jit(solution)/shard_map/all_gather | solution.py:22
  196.4 0.2 broadcast_in_dim.21
  196.7 30.3 %while.10 = (s32[]{:T(128)}, f32[8,128,512]{2,1,0:T(8,128)S(1)}, s32[]{:T(128)}, pred[8,12]{1,0:T(8,128)(4,1)S(1)}, bf16[8,12,128,128]{3,2,1,0:T(8,128)(2,1)}, /...) while((s32[]{:T(128)}, f32[8,128,512]{2,1,0:T(8,128)S(1)}, ...), condition=%wide.region_2.3_spmd, body=%wide.region_1.2_spmd.sunk | while | flops 537920640 | bytes 17830920 | solution.py:38
  196.7 0.1 compare_select_fusion.2
  196.8 0.1 reshape.32
  196.8 6.2 %gather_fusion = bf16[32,128,512]{2,1,0:T(8,128)(2,1)} fusion(bf16[64,128,512]{2,1,0:T(8,128)(2,1)} %get-tuple-element.131, s32[1024]{0:T(1024)S(1)} %pad_clamp_fusion.2), kind=kCustom, calls=%fused_computation.clone.1 | custom fusion | bytes 8388736 | tf_op jit(solution)/shard_map/while/body/gather | solution.py:33
  203.0 0.1 constant_dynamic-slice_fusion.2
  203.1 3.6 bitcast_add_fusion.2
  206.8 0.1 compare_select_fusion.2
  206.8 0.1 reshape.32
  206.9 6.2 %gather_fusion = bf16[32,128,512]{2,1,0:T(8,128)(2,1)} fusion(bf16[64,128,512]{2,1,0:T(8,128)(2,1)} %get-tuple-element.131, s32[1024]{0:T(1024)S(1)} %pad_clamp_fusion.2), kind=kCustom, calls=%fused_computation.clone.1 | custom fusion | bytes 8388736 | tf_op jit(solution)/shard_map/while/body/gather | solution.py:33
  213.1 0.1 constant_dynamic-slice_fusion.2
  213.2 3.6 bitcast_add_fusion.2
  216.9 0.1 compare_select_fusion.2
  216.9 0.1 reshape.32
  217.0 6.2 %gather_fusion = bf16[32,128,512]{2,1,0:T(8,128)(2,1)} fusion(bf16[64,128,512]{2,1,0:T(8,128)(2,1)} %get-tuple-element.131, s32[1024]{0:T(1024)S(1)} %pad_clamp_fusion.2), kind=kCustom, calls=%fused_computation.clone.1 | custom fusion | bytes 8388736 | tf_op jit(solution)/shard_map/while/body/gather | solution.py:33
  223.2 0.1 constant_dynamic-slice_fusion.2
  223.3 3.6 bitcast_add_fusion.2
  227.0 67.9 %all-reduce.4 = bf16[1024,512]{1,0:T(8,128)(2,1)} all-reduce(f32[1024,512]{1,0:T(8,128)S(1)} %bitcast.19), channel_id=1, replica_groups=mesh['section'=64,'rep'=8] {'rep'}, use_global_device_ids=true, to_apply=%region_3.4 | all-reduce | flops 524288 | bytes 3145728 | tf_op jit(solution)/shard_map/psum | solution.py:41
  294.8 1.9 convert_reduce_fusion
  296.7 2.3 fusion.6
  299.0 0.0 all-reduce.3.cloned.1.call-update
  299.0 99.1 %psum.23 = f32[512]{0:T(512)S(1)} all-reduce(f32[512]{0:T(512)S(1)} %get-tuple-element.56), channel_id=1, replica_groups=mesh['section'=64,'rep'=8] {'section','rep'}, use_global_device_ids=true, to_apply=%region_6.7 | all-reduce | flops 512 | bytes 4096 | tf_op jit(solution)/shard_map/psum | solution.py:52
  398.1 0.6 broadcast_multiply_fusion.1
  398.7 175.6 %all-reduce.3.cloned.1.call-done = f32[512,512]{1,0:T(8,128)} async-done(((f32[512,512]{1,0:T(8,128)}), f32[512,512]{1,0:T(8,128)}) %all-reduce.3.cloned.1.call-update) | async-done | bytes 1048592 | tf_op jit(solution)/shard_map/psum | solution.py:52
  574.2 2.3 broadcast_multiply_fusion
  (9 shorter events, 0.0 us)
Async XLA Ops:
  7.2 287.7 %copy-start = (bf16[512,512]{1,0:T(8,128)(2,1)S(1)}, bf16[512,512]{1,0:T(8,128)(2,1)}, u32[]{:S(2)}) copy-start(bf16[512,512]{1,0:T(8,128)(2,1)} %param.13) | copy-start | bytes 1572868
  7.2 189.2 %all-gather.2.cloned.1.call-start = ((), (), s32[]{:S(2)}) async-start(), calls=%async_computation | async-start | bytes 8519680 | tf_op jit(solution)/shard_map/all_gather | solution.py:22
  7.9 566.3 %all-reduce.3.cloned.1.call-start = ((), (), s32[]{:S(2)}) async-start(), calls=%async_computation.1 | async-start | bytes 2097152 | tf_op jit(solution)/shard_map/psum | solution.py:52
  226.9 67.9 %copy-start.1 = (bf16[128,512]{1,0:T(8,128)(2,1)S(1)}, bf16[128,512]{1,0:T(8,128)(2,1)}, u32[]{:S(2)}) copy-start(bf16[128,512]{1,0:T(8,128)(2,1)} %param.15) | copy-start | bytes 393220
  226.9 67.9 %copy-start.2 = (f32[512]{0:T(512)S(1)}, f32[512]{0:T(512)}, u32[]{:S(2)}) copy-start(f32[512]{0:T(512)} %param.14) | copy-start | bytes 6148
Sparse Core Ops, SparseCore 0:
  12.3 183.9 all-gather.1
  299.1 275.0 all-reduce.2
where the time goes:
time: 584 us; the launch traced here: 583 us
  waiting for transfers between devices  361 us (62%)
  blocking collectives  167 us (29%)
  local copies, waits for them, and re-layouts  19.3 us (3%)
  matrix products  15.1 us (3%)
  between operations  14.8 us (3%)
  other arithmetic  5.84 us (1%)
    all_gather x1, waiting for transfers between devices, shards(): gathered = lax.all_gather(features, 'section', axis=0, tiled=True)  185 us
    psum x1, waiting for transfers between devices, shards(): lax.psum((local_weight, local_bias), ('section', 'rep'))  176 us
    psum x1, blocking collectives, shards(): lax.psum((local_weight, local_bias), ('section', 'rep'))  99.1 us
    psum x1, blocking collectives, shards(): summed_all = lax.psum(partial_value, 'rep')  67.9 us
    gather x3, local copies, waits for them, and re-layouts, one_turn(): picked = all_panels[step_cols]  18.5 us
  transfers between devices with their start and end apart: 2, of which 2 were waited for; matrix products, arithmetic and copies ran while one was open for 1% of the time, Pallas kernels for 0%

commit v1 on v0

--- a/solution.py
+++ b/solution.py
@@ -19,7 +19,9 @@
     slot_mask = jnp.arange(slot_count, dtype=jnp.int32)[None, :] < live_counts[:, None]
     tiles = block_values[:, 0]
     empty = jnp.zeros((row_panels, tile_size, feat_width), jnp.float32)
-    gathered = lax.all_gather(features, "section", axis=0, tiled=True)
+    gathered = jnp.concatenate(
+        lax.all_to_all(jnp.stack([features] * lax.axis_size("section")), "section", 0, 0), axis=0
+    )
     all_panels = gathered.reshape(-1, tile_size, feat_width)
     slot_step = 4
     turn_count = (jnp.max(live_counts) + slot_step - 1) // slot_step

time: 584 us -> 656 us (1.12)
  waiting for transfers between devices: 361 us -> 412 us
  starting transfers between devices: 0.08 us -> 16.8 us
    all_to_all x0 -> x1, waiting for transfers between devices: none -> 237 us  [shards(): lax.all_to_all(jnp.stack([features] * lax.axis_size('section')), 'section...]
    all_gather x1 -> x0, waiting for transfers between devices: 185 us -> none  [shards(): gathered = lax.all_gather(features, 'section', axis=0, tiled=True)]
    all_to_all x0 -> x1, starting transfers between devices: none -> 16.7 us  [shards(): lax.all_to_all(jnp.stack([features] * lax.axis_size('section')), 'section...]
    psum x1, blocking collectives: 99.1 us -> 110 us  [shards(): lax.psum((local_weight, local_bias), ('section', 'rep'))]
    psum x1, blocking collectives: 67.9 us -> 58.5 us  [shards(): summed_all = lax.psum(partial_value, 'rep')]
  transfers between devices with their start and end apart: 2 -> 2, of which waited for: 2 -> 2; matrix products, arithmetic and copies ran while one was open for 1% -> 0% of each run, Pallas kernels for 0% -> 0%
where the time goes in v1:
time: 656 us
  waiting for transfers between devices  412 us (63%)
  blocking collectives  168 us (26%)
  local copies, waits for them, and re-layouts  24.4 us (4%)
  starting transfers between devices  16.8 us (3%)
  matrix products  15.1 us (2%)
  between operations  14.8 us (2%)
    all_to_all x1, waiting for transfers between devices, shards(): lax.all_to_all(jnp.stack([features] * lax.axis_size('section')), 'section...  237 us
    psum x1, waiting for transfers between devices, shards(): lax.psum((local_weight, local_bias), ('section', 'rep'))  176 us
    psum x1, blocking collectives, shards(): lax.psum((local_weight, local_bias), ('section', 'rep'))  110 us
    psum x1, blocking collectives, shards(): summed_all = lax.psum(partial_value, 'rep')  58.5 us
    gather x3, local copies, waits for them, and re-layouts, one_turn(): picked = all_panels[step_cols]  18.5 us
    all_to_all x1, starting transfers between devices, shards(): lax.all_to_all(jnp.stack([features] * lax.axis_size('section')), 'section...  16.7 us
  transfers between devices with their start and end apart: 2, of which 2 were waited for; matrix products, arithmetic and copies ran while one was open for 0% of the time, Pallas kernels for 0%

profile of v1, /device:TPU:24, one launch (start us, length us, event | category | flops | bytes accessed | tf_op | source)
XLA Modules:
  0.0 655.7 jit_solution(6080406406406567068)
XLA Ops:
  7.2 0.0 copy-start
  7.2 5.2 stack.2
  12.4 16.7 %all-to-all-start = ((bf16[64,128,512]{2,1,0:T(8,128)(2,1)}), bf16[64,128,512]{2,1,0:T(8,128)(2,1)}, u32[]{:S(2)}, u32[]{:S(2)}) async-start(bf16[64,128,512]{2,1,0:T(8,128)(2,1)} %stack.2), calls=%async_computation | async-start | bytes 16777216 | tf_op jit(solution)/shard_map/all_to_all | solution.py:23
  29.1 0.0 all-reduce.3.cloned.1.call-start
  29.2 0.6 reduce_max.9
  30.5 0.1 iota_compare_fusion
  30.6 236.6 %all-to-all-done = bf16[64,128,512]{2,1,0:T(8,128)(2,1)} async-done(((bf16[64,128,512]{2,1,0:T(8,128)(2,1)}), bf16[64,128,512]{2,1,0:T(8,128)(2,1)}, u32[]{:S(2)}, u32[]{:S(2)}) %all-to-all-start) | async-done | bytes 8388640 | tf_op jit(solution)/shard_map/all_to_all | solution.py:23
  267.2 0.2 broadcast_in_dim.21
  267.4 30.3 %while.10 = (s32[]{:T(128)}, f32[8,128,512]{2,1,0:T(8,128)S(1)}, s32[]{:T(128)}, pred[8,12]{1,0:T(8,128)(4,1)S(1)}, bf16[8,12,128,128]{3,2,1,0:T(8,128)(2,1)}, /...) while((s32[]{:T(128)}, f32[8,128,512]{2,1,0:T(8,128)S(1)}, ...), condition=%wide.region_2.3_spmd, body=%wide.region_1.2_spmd.sunk | while | flops 537920640 | bytes 17830920 | solution.py:40
  267.5 0.1 compare_select_fusion.2
  267.5 0.1 reshape.30
  267.6 6.2 gather_fusion
  273.8 0.1 constant_dynamic-slice_fusion.2
  273.9 3.6 bitcast_add_fusion.2
  277.6 0.1 compare_select_fusion.2
  277.6 0.1 reshape.30
  277.7 6.2 gather_fusion
  283.9 0.1 constant_dynamic-slice_fusion.2
  284.0 3.6 bitcast_add_fusion.2
  287.6 0.1 compare_select_fusion.2
  287.7 0.1 reshape.30
  287.8 6.2 gather_fusion
  294.0 0.1 constant_dynamic-slice_fusion.2
  294.1 3.6 bitcast_add_fusion.2
  297.7 58.5 %all-reduce.4 = bf16[1024,512]{1,0:T(8,128)(2,1)} all-reduce(f32[1024,512]{1,0:T(8,128)S(1)} %bitcast.18), channel_id=1, replica_groups=mesh['section'=64,'rep'=8] {'rep'}, use_global_device_ids=true, to_apply=%region_3.4 | all-reduce | flops 524288 | bytes 3145728 | tf_op jit(solution)/shard_map/psum | solution.py:43
  356.3 1.9 convert_reduce_fusion
  358.2 2.3 fusion.6
  360.4 0.0 all-reduce.3.cloned.1.call-update
  360.5 109.9 %psum.23 = f32[512]{0:T(512)S(1)} all-reduce(f32[512]{0:T(512)S(1)} %get-tuple-element.56), channel_id=1, replica_groups=mesh['section'=64,'rep'=8] {'section','rep'}, use_global_device_ids=true, to_apply=%region_6.7 | all-reduce | flops 512 | bytes 4096 | tf_op jit(solution)/shard_map/psum | solution.py:54
  470.4 0.6 broadcast_multiply_fusion.1
  471.0 175.6 %all-reduce.3.cloned.1.call-done = f32[512,512]{1,0:T(8,128)} async-done(((f32[512,512]{1,0:T(8,128)}), f32[512,512]{1,0:T(8,128)}) %all-reduce.3.cloned.1.call-update) | async-done | bytes 1048592 | tf_op jit(solution)/shard_map/psum | solution.py:54
  646.5 2.3 broadcast_multiply_fusion
  (13 shorter events, 0.1 us)
Async XLA Ops:
  7.2 349.1 %copy-start = (bf16[512,512]{1,0:T(8,128)(2,1)S(1)}, bf16[512,512]{1,0:T(8,128)(2,1)}, u32[]{:S(2)}) copy-start(bf16[512,512]{1,0:T(8,128)(2,1)} %param.13) | copy-start | bytes 1572868
  12.4 16.8 %copy-start.4 = (s32[8,1]{0,1:T(1,128)S(1)}, s32[8,1]{0,1:T(1,128)}, u32[]{:S(2)}) copy-start(s32[8,1]{0,1:T(1,128)} %param.11) | copy-start | bytes 100
  12.4 18.2 %copy-start.1 = (s32[8,1,12]{2,1,0:T(1,128)S(1)}, s32[8,1,12]{2,1,0:T(1,128)}, u32[]{:S(2)}) copy-start(s32[8,1,12]{2,1,0:T(1,128)} %param.10) | copy-start | bytes 1156
  12.4 254.8 %all-to-all-start = ((bf16[64,128,512]{2,1,0:T(8,128)(2,1)}), bf16[64,128,512]{2,1,0:T(8,128)(2,1)}, u32[]{:S(2)}, u32[]{:S(2)}) async-start(bf16[64,128,512]{2,1,0:T(8,128)(2,1)} %stack.2), calls=%async_computation | async-start | bytes 16777216 | tf_op jit(solution)/shard_map/all_to_all | solution.py:23
  29.1 617.4 %all-reduce.3.cloned.1.call-start = ((), (), s32[]{:S(2)}) async-start(), calls=%async_computation.1 | async-start | bytes 2097152 | tf_op jit(solution)/shard_map/psum | solution.py:54
  297.7 58.6 %copy-start.2 = (bf16[128,512]{1,0:T(8,128)(2,1)S(1)}, bf16[128,512]{1,0:T(8,128)(2,1)}, u32[]{:S(2)}) copy-start(bf16[128,512]{1,0:T(8,128)(2,1)} %param.15) | copy-start | bytes 393220
  297.7 58.6 %copy-start.3 = (f32[512]{0:T(512)S(1)}, f32[512]{0:T(512)}, u32[]{:S(2)}) copy-start(f32[512]{0:T(512)} %param.14) | copy-start | bytes 6148
Sparse Core Ops, SparseCore 0:
  360.6 285.8 all-reduce.2

commit v2 on v0

--- a/solution.py
+++ b/solution.py
@@ -38,7 +38,7 @@
     gathered_sum = lax.fori_loop(0, turn_count, one_turn, empty)
     partial_value = gathered_sum.reshape(row_panels * tile_size, feat_width)
     own_rows = own_panels * tile_size
-    summed_all = lax.psum(partial_value, "rep")
+    summed_all = jnp.sum(lax.all_gather(partial_value, "rep"), axis=0)
     summed_own = lax.dynamic_slice_in_dim(summed_all, rep_index * own_rows, own_rows, 0)
     aggregated = summed_own.astype(jnp.bfloat16)
     pre = jnp.dot(aggregated, weight, preferred_element_type=jnp.float32) + bias

time: 584 us -> 703 us (1.20)
  waiting for transfers between devices: 361 us -> 540 us
  blocking collectives: 167 us -> 101 us
  other arithmetic: 5.84 us -> 13.9 us
    all_gather x0 -> x1, waiting for transfers between devices: none -> 177 us  [shards(): summed_all = jnp.sum(lax.all_gather(partial_value, 'rep'), axis=0)]
    psum x1 -> x0, blocking collectives: 67.9 us -> none  [shards(): summed_all = lax.psum(partial_value, 'rep')]
    reduce_sum x0 -> x1, other arithmetic: none -> 8.09 us  [shards(): summed_all = jnp.sum(lax.all_gather(partial_value, 'rep'), axis=0)]
  transfers between devices with their start and end apart: 2 -> 3, of which waited for: 2 -> 3; matrix products, arithmetic and copies ran while one was open for 1% -> 0% of each run, Pallas kernels for 0% -> 0%
where the time goes in v2:
time: 703 us
  waiting for transfers between devices  540 us (77%)
  blocking collectives  101 us (14%)
  local copies, waits for them, and re-layouts  20.6 us (3%)
  between operations  14.5 us (2%)
  other arithmetic  13.9 us (2%)
  matrix products  13.2 us (2%)
    all_gather x1, waiting for transfers between devices, shards(): gathered = lax.all_gather(features, 'section', axis=0, tiled=True)  185 us
    psum x1, waiting for transfers between devices, shards(): lax.psum((local_weight, local_bias), ('section', 'rep'))  177 us
    all_gather x1, waiting for transfers between devices, shards(): summed_all = jnp.sum(lax.all_gather(partial_value, 'rep'), axis=0)  177 us
    psum x1, blocking collectives, shards(): lax.psum((local_weight, local_bias), ('section', 'rep'))  101 us
    gather x3, local copies, waits for them, and re-layouts, one_turn(): picked = all_panels[step_cols]  18.5 us
  transfers between devices with their start and end apart: 3, of which 3 were waited for; matrix products, arithmetic and copies ran while one was open for 0% of the time, Pallas kernels for 0%

profile of v2, /device:TPU:24, one launch (start us, length us, event | category | flops | bytes accessed | tf_op | source)
XLA Modules:
  0.0 702.6 jit_solution(7923130414993340645)
XLA Ops:
  7.2 0.7 all-gather.3.cloned.1.call-update
  8.0 1.3 reduce_max.9
  9.9 0.7 iota_compare_fusion
  10.7 0.7 add_select_fusion
  11.4 185.0 %all-gather.3.cloned.1.call-done = bf16[8192,512]{1,0:T(8,128)(2,1)} async-done(((bf16[128,512]{1,0:T(8,128)(2,1)}), bf16[8192,512]{1,0:T(8,128)(2,1)}) %all-gather.3.cloned.1.call-update) | async-done | bytes 8388624 | tf_op jit(solution)/shard_map/all_gather | solution.py:22
  196.4 0.2 broadcast_in_dim.21
  196.7 30.3 %while.10 = (s32[]{:T(128)}, f32[8,128,512]{2,1,0:T(8,128)S(1)}, s32[]{:T(128)}, pred[8,12]{1,0:T(8,128)(4,1)S(1)}, bf16[8,12,128,128]{3,2,1,0:T(8,128)(2,1)}, /...) while((s32[]{:T(128)}, f32[8,128,512]{2,1,0:T(8,128)S(1)}, ...), condition=%wide.region_2.3_spmd, body=%wide.region_1.2_spmd.sunk | while | flops 537920640 | bytes 17830920 | solution.py:38
  196.7 0.1 compare_select_fusion.2
  196.8 0.1 reshape.28
  196.9 6.2 gather_fusion
  203.0 0.1 constant_dynamic-slice_fusion.2
  203.1 3.6 bitcast_add_fusion.2
  206.8 0.1 compare_select_fusion.2
  206.9 0.1 reshape.28
  206.9 6.2 gather_fusion
  213.1 0.1 constant_dynamic-slice_fusion.2
  213.2 3.6 bitcast_add_fusion.2
  216.9 0.1 compare_select_fusion.2
  216.9 0.1 reshape.28
  217.0 6.2 gather_fusion
  223.2 0.1 constant_dynamic-slice_fusion.2
  223.3 3.7 bitcast_add_fusion.2
  227.0 1.3 copy-done.1
  228.3 0.0 all-reduce.2.cloned.1.call-start
  228.4 176.7 %all-gather.5.cloned.1.call-done = f32[8,1024,512]{2,1,0:T(8,128)} async-done(((f32[1,1024,512]{2,1,0:T(8,128)}), f32[8,1024,512]{2,1,0:T(8,128)}) %all-gather.5.cloned.1.call-update) | async-done | bytes 16777232 | tf_op jit(solution)/shard_map/all_gather | solution.py:41
  405.1 8.1 %reduce_sum.18 = bf16[1024,512]{1,0:T(8,128)(2,1)S(1)} reduce(f32[8,1024,512]{2,1,0:T(8,128)} %all-gather.5.cloned.1.call-done, f32[]{:T(128)} %constant.65.clone.1), dimensions={0}, to_apply=%region_3.4 | reduce | flops 3670016 | bytes 17825796 | tf_op jit(solution)/shard_map/reduce_sum | solution.py:41
  413.2 1.0 convert_reduce_fusion
  414.2 1.3 fusion.6
  415.5 100.6 %psum.15 = f32[512]{0:T(512)S(1)} all-reduce(f32[512]{0:T(512)S(1)} %get-tuple-element.56), channel_id=1, replica_groups=mesh['section'=64,'rep'=8] {'section','rep'}, use_global_device_ids=true, to_apply=%region_6.7 | all-reduce | flops 512 | bytes 4096 | tf_op jit(solution)/shard_map/psum | solution.py:52
  516.1 0.6 broadcast_multiply_fusion.1
  516.6 177.1 %all-reduce.2.cloned.1.call-done = f32[512,512]{1,0:T(8,128)} async-done(((f32[512,512]{1,0:T(8,128)}), f32[512,512]{1,0:T(8,128)}) %all-reduce.2.cloned.1.call-update) | async-done | bytes 1048592 | tf_op jit(solution)/shard_map/psum | solution.py:52
  693.7 2.3 broadcast_multiply_fusion
  (14 shorter events, 0.2 us)
Async XLA Ops:
  7.2 406.0 %copy-start = (bf16[512,512]{1,0:T(8,128)(2,1)S(1)}, bf16[512,512]{1,0:T(8,128)(2,1)}, u32[]{:S(2)}) copy-start(bf16[512,512]{1,0:T(8,128)(2,1)} %param.13) | copy-start | bytes 1572868
  7.2 189.2 %all-gather.3.cloned.1.call-start = ((), (), s32[]{:S(2)}) async-start(), calls=%async_computation | async-start | bytes 8519680 | tf_op jit(solution)/shard_map/all_gather | solution.py:22
  7.9 397.1 %all-gather.5.cloned.1.call-start = ((), (), s32[]{:S(2)}) async-start(), calls=%async_computation.1 | async-start | bytes 18874368 | tf_op jit(solution)/shard_map/all_gather | solution.py:41
  227.0 1.3 copy-start.1
  228.3 465.4 %all-reduce.2.cloned.1.call-start = ((), (), s32[]{:S(2)}) async-start(), calls=%async_computation.2 | async-start | bytes 2097152 | tf_op jit(solution)/shard_map/psum | solution.py:52
  228.4 184.8 %copy-start.2 = (bf16[128,512]{1,0:T(8,128)(2,1)S(1)}, bf16[128,512]{1,0:T(8,128)(2,1)}, u32[]{:S(2)}) copy-start(bf16[128,512]{1,0:T(8,128)(2,1)} %param.15) | copy-start | bytes 393220
  228.4 184.8 %copy-start.3 = (f32[512]{0:T(512)S(1)}, f32[512]{0:T(512)}, u32[]{:S(2)}) copy-start(f32[512]{0:T(512)} %param.14) | copy-start | bytes 6148
Sparse Core Ops, SparseCore 0:
  12.3 184.0 all-gather.2
  228.4 176.5 all-gather.4
  415.6 278.0 all-reduce.1
